TPU v7x, 128 devices: a whole 4x4x4 slice. The times are simulated.
128 devices in a mesh: gx: 32 (over x, z, core), dev: 4 (over y).
Axes of the slice: x: 4, y: 4, z: 4, core: 2. Of those that a mesh axis runs over, the one named last changes fastest.
Arguments:
- densities: float32 [8, 192, 256, 256], P('dev', 'gx'), may hold values from 0.05 to 2000, as said below
- raw_weights: float32 [8], replicated, may hold values from 0.5 to 2
Outputs:
- barycenter: float32 [192, 256, 256], P('gx')
- scalings: float32 [8, 192, 256, 256], P('dev', 'gx')
Inputs may be any that keep to these rules, and one draw needn't show every extreme that they name: `densities`: every entry is positive.
All inputs are finite; a program needn't handle non-finite values.
Results may differ from a plain program's by a relative error of at most 0.000043.
Values sent between devices are 32-bit elements; how exact they have to be, the bound alone decides.
No kernel may reach another device: no remote copies, remote signals or barrier semaphores. Data moves between devices by JAX's collectives and lax.ppermute only.
A program may use at most 64 MiB of HBM per device.

v0:
```python
import jax
import jax.numpy as jnp
import numpy as np
from jax import lax
from jax.sharding import PartitionSpec as P

ITERS = 2


gauss_raw = np.exp(-np.arange(-6, 7) ** 2 / 12.5)
gauss_taps = [float(value) for value in gauss_raw / gauss_raw.sum()]


def padded_2(cells, sides, width):
    for axis, dim in sides:
        count = lax.axis_size(axis)
        ends = count - 1
        head = lax.slice_in_dim(cells, 0, width, axis=dim)
        tail = lax.slice_in_dim(cells, cells.shape[dim] - width, cells.shape[dim], axis=dim)
        cells = jnp.concatenate(
            [
                lax.ppermute(tail, axis, [(i, (i + 1) % count) for i in range(ends)]),
                cells,
                lax.ppermute(head, axis, [((i + 1) % count, i) for i in range(ends)]),
            ],
            axis=dim,
        )
    return cells


def taps_over(padded, axis, length):
    total = gauss_taps[0] * lax.slice_in_dim(padded, 0, length, axis=axis)
    for index in range(1, len(gauss_taps)):
        total = total + gauss_taps[index] * lax.slice_in_dim(
            padded, index, index + length, axis=axis
        )
    return total


def pad_axis(field, axis):
    reach = len(gauss_taps) // 2
    widths = [(0, 0)] * field.ndim
    widths[axis] = (reach, reach)
    return jnp.pad(field, widths)


def heat_blur(field):
    reach = len(gauss_taps) // 2
    planes = field.shape[1]
    padded = padded_2(field, (("gx", 1),), reach)
    along = taps_over(padded, 1, planes)
    along = taps_over(pad_axis(along, 2), 2, along.shape[2])
    return taps_over(pad_axis(along, 3), 3, along.shape[3])


def per_device(densities, raw_weights):
    local_count = densities.shape[0]
    count = raw_weights.shape[0]
    lam = raw_weights / jnp.sum(raw_weights)
    offset = lax.axis_index("dev") * local_count
    lam_local = lax.dynamic_slice_in_dim(lam, offset, local_count)
    cells = densities.shape[1] * lax.axis_size("gx") * densities.shape[2] * densities.shape[3]
    placing = (jnp.arange(count)[:, None] == (offset + jnp.arange(local_count))[None, :]).astype(
        jnp.float32
    )
    local_sums = jnp.sum(densities, axis=(1, 2, 3))
    totals = lax.psum(jnp.sum(placing * local_sums[None, :], axis=1), ("gx", "dev"))
    mean_local = lax.dynamic_slice_in_dim(totals / cells, offset, local_count)
    field = densities / mean_local[:, None, None, None]
    scal = jnp.ones(densities.shape, jnp.float32)
    barycenter = scal[0]
    rounds = 0
    for step in range(ITERS):
        wfield = field / heat_blur(scal)
        dfield = scal * heat_blur(wfield)
        partial_log = jnp.sum(lam_local[:, None, None, None] * jnp.log(dfield), axis=0)
        barycenter = jnp.exp(lax.psum(partial_log, "dev"))
        scal = scal * barycenter[None] / dfield
        rounds = rounds + 1
    return (barycenter, scal)


def solution(mesh):
    in_specs = (P("dev", "gx", None, None), P())
    out_specs = (P("gx", None, None), P("dev", "gx", None, None))
    return jax.shard_map(
        per_device, mesh=mesh, in_specs=in_specs, out_specs=out_specs, check_vma=False
    )
```

profile of v0, /device:TPU:1, one launch (start us, length us, event | category | flops | bytes accessed | tf_op | source)
XLA Modules:
  0.0 465.5 jit_solution(12727851226378632982)
XLA Ops:
  9.2 3.4 collective-permute-start.1
  12.6 3.6 collective-permute-start
  16.8 95.7 %psum.21 = f32[8]{0:T(128)S(1)} all-reduce(f32[8]{0:T(128)S(1)} %fusion.249), channel_id=1, replica_groups=mesh['gx'=32,'dev'=4] {'gx','dev'}, use_global_device_ids=true, to_apply=%region_3.0 | all-reduce | flops 8 | bytes 64 | tf_op jit(solution)/shard_map/psum | solution.py:67
  112.6 10.9 %fusion.197 = f32[2,6,256,256]{3,2,1,0:T(8,128)S(1)} fusion(f32[2,6,256,256]{3,2,1,0:T(8,128)} %collective-permute-done, f32[2,6,256,256]{3,2,1,0:T(8,128)} %collective-permute-done.1), kind=kLoop, calls=%fused_computation.303 | loop fusion | flops 18874368 | bytes 9437184 | tf_op jit(solution)/shard_map/add | solution.py:34
  123.5 5.0 %multiply_add_fusion.3 = f32[2,6,256,256]{3,2,1,0:T(8,128)S(1)} fusion(f32[2,6,256,256]{3,2,1,0:T(8,128)S(1)} %fusion.197), kind=kLoop, calls=%fused_computation.373 | loop fusion | flops 19660800 | bytes 6291456 | tf_op jit(solution)/shard_map/add | solution.py:34
  128.6 11.1 %fusion.98 = f32[2,6,256,256]{3,2,1,0:T(8,128)} fusion(f32[2,6,256,256]{3,2,1,0:T(8,128)S(1)} %copy-done, f32[2,6,256,256]{3,2,1,0:T(8,128)S(1)} %multiply_add_fusion.3, f32[2]{0:T(128)S(1)} %dynamic_slice.7), kind=kLoop, calls=%fused_computation.204 | loop fusion | flops 21233664 | bytes 9437192 | tf_op jit(solution)/shard_map/div | solution.py:74
  142.4 3.0 collective-permute-start.2
  146.8 31.8 %collective-permute-done.3 = f32[2,6,256,256]{3,2,1,0:T(8,128)} collective-permute-done((f32[2,6,256,256]{3,2,1,0:T(8,128)}, f32[2,6,256,256]{3,2,1,0:T(8,128)}, u32[]{:S(2)}, u32[]{:S(2)}) %collective-permute-start.3) | collective-permute-done | bytes 3145760 | tf_op jit(solution)/shard_map/ppermute | solution.py:24
  179.8 15.5 %fusion.60 = f32[2,6,256,256]{3,2,1,0:T(8,128)S(1)} fusion(f32[2,6,256,256]{3,2,1,0:T(8,128)} %fusion.98, f32[2,6,256,256]{3,2,1,0:T(8,128)} %collective-permute-done.3, f32[2,6,256,256]{3,2,1,0:T(8,128)} %collective-permute-done.2), kind=kLoop, calls=%fused_computation.166 | loop fusion | flops 27525120 | bytes 12582912 | tf_op jit(solution)/shard_map/add | solution.py:34
  195.3 5.0 %multiply_add_fusion.2 = f32[2,6,256,256]{3,2,1,0:T(8,128)S(1)} fusion(f32[2,6,256,256]{3,2,1,0:T(8,128)S(1)} %fusion.60), kind=kLoop, calls=%fused_computation.358 | loop fusion | flops 19660800 | bytes 6291456 | tf_op jit(solution)/shard_map/add | solution.py:34
  200.3 11.2 %multiply_reduce_fusion.1 = (f32[6,256,256]{2,1,0:T(8,128)}, f32[2,6,256,256]{3,2,1,0:T(8,128)S(1)}) fusion(f32[2]{0:T(128)S(1)} %dynamic_slice.6, f32[2,6,256,256]{3,2,1,0:T(8,128)S(1)} %multiply_add_fusion.2), kind=kLoop, calls=%fused_computation.357 | loop fusion | flops 20840448 | bytes 7864328 | tf_op jit(solution)/shard_map/reduce_sum | solution.py:76
  211.6 50.4 %all-reduce.13.cloned.1.call-done = f32[6,256,256]{2,1,0:T(8,128)} async-done(((f32[6,256,256]{2,1,0:T(8,128)}), f32[6,256,256]{2,1,0:T(8,128)}) %all-reduce.13.cloned.1.call-update) | async-done | bytes 1572880 | tf_op jit(solution)/shard_map/psum | solution.py:77
  266.9 3.3 collective-permute-start.4
  270.3 32.8 %collective-permute-done.5 = f32[2,6,256,256]{3,2,1,0:T(8,128)S(1)} collective-permute-done((f32[2,6,256,256]{3,2,1,0:T(8,128)S(1)}, f32[2,6,256,256]{3,2,1,0:T(8,128)S(1)}, u32[]{:S(2)}, u32[]{:S(2)}) %collective-permute-start.5) | collective-permute-done | bytes 3145760 | tf_op jit(solution)/shard_map/ppermute | solution.py:24
  304.2 3.6 fusion.32
  307.8 6.0 %multiply_add_fusion.1 = f32[2,6,256,256]{3,2,1,0:T(8,128)} fusion(f32[2,6,256,256]{3,2,1,0:T(8,128)S(1)} %fusion.32), kind=kLoop, calls=%fused_computation.342 | loop fusion | flops 19660800 | bytes 6291456 | tf_op jit(solution)/shard_map/add | solution.py:34
  313.8 21.1 %fusion.148 = f32[2,6,256,256]{3,2,1,0:T(8,128)S(1)} fusion(f32[2,6,256,256]{3,2,1,0:T(8,128)S(1)} %copy-done.1, f32[2,6,256,256]{3,2,1,0:T(8,128)} %multiply_add_fusion.1, f32[2]{0:T(128)S(1)} %dynamic_slice.7), kind=kLoop, calls=%fused_computation.254 | loop fusion | flops 21233664 | bytes 9437192 | tf_op jit(solution)/shard_map/div | solution.py:74
  336.8 4.6 collective-permute-start.6
  341.5 32.7 %collective-permute-done.7 = f32[2,6,256,256]{3,2,1,0:T(8,128)S(1)} collective-permute-done((f32[2,6,256,256]{3,2,1,0:T(8,128)S(1)}, f32[2,6,256,256]{3,2,1,0:T(8,128)S(1)}, u32[]{:S(2)}, u32[]{:S(2)}) %collective-permute-start.7) | collective-permute-done | bytes 3145760 | tf_op jit(solution)/shard_map/ppermute | solution.py:24
  375.4 4.6 fusion.4
  380.0 5.0 %multiply_add_fusion = f32[2,6,256,256]{3,2,1,0:T(8,128)S(1)} fusion(f32[2,6,256,256]{3,2,1,0:T(8,128)S(1)} %fusion.4), kind=kLoop, calls=%fused_computation.327 | loop fusion | flops 19660800 | bytes 6291456 | tf_op jit(solution)/shard_map/add | solution.py:34
  385.0 12.3 %multiply_reduce_fusion = (f32[6,256,256]{2,1,0:T(8,128)}, f32[2,6,256,256]{3,2,1,0:T(8,128)}) fusion(f32[2]{0:T(128)S(1)} %dynamic_slice.6, f32[2,6,256,256]{3,2,1,0:T(8,128)S(1)} %multiply_add_fusion, f32[2,6,256,256]{3,2,1,0:T(8,128)S(1)} %get-tuple-element.5, f32[6,256,256]{2,1,0:T(8,128)S(1)} %exp.6), kind=kLoop, calls=%fused_computation.326 | loop fusion | flops 22413312 | bytes 12582920 | tf_op jit(solution)/shard_map/reduce_sum | solution.py:76
  397.3 54.6 %all-reduce.15.cloned.1.call-done = f32[6,256,256]{2,1,0:T(8,128)} async-done(((f32[6,256,256]{2,1,0:T(8,128)}), f32[6,256,256]{2,1,0:T(8,128)}) %all-reduce.15.cloned.1.call-update) | async-done | bytes 1572880 | tf_op jit(solution)/shard_map/psum | solution.py:77
  453.8 4.8 %multiply_divide_fusion = f32[2,6,256,256]{3,2,1,0:T(8,128)} fusion(f32[2,6,256,256]{3,2,1,0:T(8,128)} %get-tuple-element.3, f32[6,256,256]{2,1,0:T(8,128)S(1)} %exp.7, f32[2,6,256,256]{3,2,1,0:T(8,128)S(1)} %get-tuple-element.5, f32[6,256,256]{2,1,0:T(8,128)S(1)} %copy-done.3), kind=kLoop, calls=%fused_computation.325 | loop fusion | flops 2359296 | bytes 12582912 | tf_op jit(solution)/shard_map/div | solution.py:78
  (36 shorter events, 19.1 us)
Async XLA Ops:
  7.2 9.0 %copy-start = (f32[2,6,256,256]{3,2,1,0:T(8,128)S(1)}, f32[2,6,256,256]{3,2,1,0:T(8,128)}, u32[]{:S(2)}) copy-start(f32[2,6,256,256]{3,2,1,0:T(8,128)} %param.2) | copy-start | bytes 9437188
  7.2 254.8 %all-reduce.13.cloned.1.call-start = ((), (), s32[]{:S(2)}) async-start(), calls=%async_computation | async-start | bytes 3145728 | tf_op jit(solution)/shard_map/psum | solution.py:77
  9.2 103.4 %collective-permute-start.1 = (f32[2,6,256,256]{3,2,1,0:T(8,128)}, f32[2,6,256,256]{3,2,1,0:T(8,128)}, u32[]{:S(2)}, u32[]{:S(2)}) collective-permute-start(f32[2,6,256,256]{3,2,1,0:T(8,128)} %broadcast_in_dim.2), channel_id=1, source_target_pairs={{4,0},{8,4},{12,8},{16,12},{20,16},{24,20},{28,24},{32,28},{36,32}... | collective-permute-start | bytes 9437192 | tf_op jit(solution)/shard_map/ppermute | solution.py:24
  12.6 100.0 %collective-permute-start = (f32[2,6,256,256]{3,2,1,0:T(8,128)}, f32[2,6,256,256]{3,2,1,0:T(8,128)}, u32[]{:S(2)}, u32[]{:S(2)}) collective-permute-start(f32[2,6,256,256]{3,2,1,0:T(8,128)} %broadcast_in_dim.2), channel_id=1, source_target_pairs={{0,4},{4,8},{8,12},{12,16},{16,20},{20,24},{24,28},{28,32},{32,36}... | collective-permute-start | bytes 9437192 | tf_op jit(solution)/shard_map/ppermute | solution.py:22
  128.6 16.9 %copy-start.5 = (f32[8]{0:T(128)S(1)}, f32[8]{0:T(128)}, u32[]{:S(2)}) copy-start(f32[8]{0:T(128)} %param.3) | copy-start | bytes 100
  139.7 38.9 %collective-permute-start.3 = (f32[2,6,256,256]{3,2,1,0:T(8,128)}, f32[2,6,256,256]{3,2,1,0:T(8,128)}, u32[]{:S(2)}, u32[]{:S(2)}) collective-permute-start(f32[2,6,256,256]{3,2,1,0:T(8,128)} %fusion.98), channel_id=1, source_target_pairs={{4,0},{8,4},{12,8},{16,12},{20,16},{24,20},{28,24},{32,28},{36,32}... | collective-permute-start | bytes 9437192 | tf_op jit(solution)/shard_map/ppermute | solution.py:24
  142.4 37.3 %collective-permute-start.2 = (f32[2,6,256,256]{3,2,1,0:T(8,128)}, f32[2,6,256,256]{3,2,1,0:T(8,128)}, u32[]{:S(2)}, u32[]{:S(2)}) collective-permute-start(f32[2,6,256,256]{3,2,1,0:T(8,128)} %fusion.98), channel_id=1, source_target_pairs={{0,4},{4,8},{8,12},{12,16},{16,20},{20,24},{24,28},{28,32},{32,36}... | collective-permute-start | bytes 9437192 | tf_op jit(solution)/shard_map/ppermute | solution.py:22
  211.6 240.4 %all-reduce.15.cloned.1.call-start = ((), (), s32[]{:S(2)}) async-start(), calls=%async_computation.1 | async-start | bytes 3145728 | tf_op jit(solution)/shard_map/psum | solution.py:77
  263.6 121.4 %copy-start.2 = (f32[6,256,256]{2,1,0:T(8,128)}, f32[6,256,256]{2,1,0:T(8,128)S(1)}, u32[]{:S(2)}) copy-start(f32[6,256,256]{2,1,0:T(8,128)S(1)} %exp.6) | copy-start | bytes 4718596
  264.3 38.8 %collective-permute-start.5 = (f32[2,6,256,256]{3,2,1,0:T(8,128)S(1)}, f32[2,6,256,256]{3,2,1,0:T(8,128)S(1)}, u32[]{:S(2)}, u32[]{:S(2)}) collective-permute-start(f32[2,6,256,256]{3,2,1,0:T(8,128)S(1)} %broadcast_divide_fusion), channel_id=1, source_target_pairs={{4,0},{8,4},{12,8},{16,12},{20,16},{24,20},{28,24},{32,28},{36,32}... | collective-permute-start | bytes 9437192 | tf_op jit(solution)/shard_map/ppermute | solution.py:24
  266.9 37.3 %collective-permute-start.4 = (f32[2,6,256,256]{3,2,1,0:T(8,128)S(1)}, f32[2,6,256,256]{3,2,1,0:T(8,128)S(1)}, u32[]{:S(2)}, u32[]{:S(2)}) collective-permute-start(f32[2,6,256,256]{3,2,1,0:T(8,128)S(1)} %broadcast_divide_fusion), channel_id=1, source_target_pairs={{0,4},{4,8},{8,12},{12,16},{16,20},{20,24},{24,28},{28,32},{32,36}... | collective-permute-start | bytes 9437192 | tf_op jit(solution)/shard_map/ppermute | solution.py:22
  307.8 6.0 %copy-start.1 = (f32[2,6,256,256]{3,2,1,0:T(8,128)S(1)}, f32[2,6,256,256]{3,2,1,0:T(8,128)}, u32[]{:S(2)}) copy-start(f32[2,6,256,256]{3,2,1,0:T(8,128)} %param.2) | copy-start | bytes 9437188
  334.9 39.3 %collective-permute-start.7 = (f32[2,6,256,256]{3,2,1,0:T(8,128)S(1)}, f32[2,6,256,256]{3,2,1,0:T(8,128)S(1)}, u32[]{:S(2)}, u32[]{:S(2)}) collective-permute-start(f32[2,6,256,256]{3,2,1,0:T(8,128)S(1)} %fusion.148), channel_id=1, source_target_pairs={{4,0},{8,4},{12,8},{16,12},{20,16},{24,20},{28,24},{32,28},{36,32}... | collective-permute-start | bytes 9437192 | tf_op jit(solution)/shard_map/ppermute | solution.py:24
  336.8 38.6 %collective-permute-start.6 = (f32[2,6,256,256]{3,2,1,0:T(8,128)S(1)}, f32[2,6,256,256]{3,2,1,0:T(8,128)S(1)}, u32[]{:S(2)}, u32[]{:S(2)}) collective-permute-start(f32[2,6,256,256]{3,2,1,0:T(8,128)S(1)} %fusion.148), channel_id=1, source_target_pairs={{0,4},{4,8},{8,12},{12,16},{16,20},{20,24},{24,28},{28,32},{32,36}... | collective-permute-start | bytes 9437192 | tf_op jit(solution)/shard_map/ppermute | solution.py:22
  452.0 1.9 copy-start.3
  453.7 5.0 %copy-start.4 = (f32[6,256,256]{2,1,0:T(8,128)}, f32[6,256,256]{2,1,0:T(8,128)S(1)}, u32[]{:S(2)}) copy-start(f32[6,256,256]{2,1,0:T(8,128)S(1)} %exp.7) | copy-start | bytes 4718596
Sparse Core Ops, SparseCore 0:
  211.7 50.2 all-reduce.12
  397.5 54.4 all-reduce.14
where the time goes:
time: 466 us; the launch traced here: 465 us
  waiting for transfers between devices  206 us (44%)
  other arithmetic  119 us (26%)
  blocking collectives  95.7 us (21%)
  starting transfers between devices  25.3 us (5%)
  between operations  14.3 us (3%)
  local copies, waits for them, and re-layouts  5.64 us (1%)
    psum x2, waiting for transfers between devices, per_device(): barycenter = jnp.exp(lax.psum(partial_log, 'dev'))  105 us
    ppermute x4, waiting for transfers between devices, padded_2(): lax.ppermute(head, axis, [((i + 1) % count, i) for i in range(ends)])  97.3 us
    psum x1, blocking collectives, per_device(): lax.psum(jnp.sum(placing * local_sums[None, :], axis=1), ('gx', 'dev'))  95.7 us
    add x8, other arithmetic, taps_over(): total + gauss_taps[index] * lax.slice_in_dim(padded, index, index + lengt...  55.7 us
    div x2, other arithmetic, per_device(): wfield = field / heat_blur(scal)  32.2 us
    reduce_sum x2, other arithmetic, per_device(): jnp.sum(lam_local[:, None, None, None] * jnp.log(dfield), axis=0)  23.5 us
    ppermute x4, starting transfers between devices, padded_2(): lax.ppermute(tail, axis, [(i, (i + 1) % count) for i in range(ends)])  14.5 us
    ppermute x4, starting transfers between devices, padded_2(): lax.ppermute(head, axis, [((i + 1) % count, i) for i in range(ends)])  10.7 us
  transfers between devices with their start and end apart: 10, of which 8 were waited for; matrix products, arithmetic and copies ran while one was open for 0% of the time, Pallas kernels for 0%

commit v1 on v0

--- a/solution.py
+++ b/solution.py
@@ -53,30 +53,47 @@
     return taps_over(pad_axis(along, 3), 3, along.shape[3])
 
 
+def ones_profile(length):
+    reach = len(gauss_taps) // 2
+    out = np.zeros(length, np.float32)
+    for position in range(length):
+        acc = np.float32(0.0)
+        for index, tap in enumerate(gauss_taps):
+            source = position + index - reach
+            if 0 <= source < length:
+                acc = acc + np.float32(tap)
+        out[position] = acc
+    return out
+
+
 def per_device(densities, raw_weights):
     local_count = densities.shape[0]
-    count = raw_weights.shape[0]
+    planes = densities.shape[1]
     lam = raw_weights / jnp.sum(raw_weights)
     offset = lax.axis_index("dev") * local_count
     lam_local = lax.dynamic_slice_in_dim(lam, offset, local_count)
-    cells = densities.shape[1] * lax.axis_size("gx") * densities.shape[2] * densities.shape[3]
-    placing = (jnp.arange(count)[:, None] == (offset + jnp.arange(local_count))[None, :]).astype(
-        jnp.float32
+    total_planes = planes * lax.axis_size("gx")
+    cells = total_planes * densities.shape[2] * densities.shape[3]
+    local_sums = jnp.sum(densities, axis=(1, 2, 3))
+    mass = lax.psum(local_sums, "gx") / cells
+    profile_x = lax.dynamic_slice_in_dim(
+        jnp.asarray(ones_profile(total_planes)), lax.axis_index("gx") * planes, planes
     )
-    local_sums = jnp.sum(densities, axis=(1, 2, 3))
-    totals = lax.psum(jnp.sum(placing * local_sums[None, :], axis=1), ("gx", "dev"))
-    mean_local = lax.dynamic_slice_in_dim(totals / cells, offset, local_count)
-    field = densities / mean_local[:, None, None, None]
-    scal = jnp.ones(densities.shape, jnp.float32)
-    barycenter = scal[0]
-    rounds = 0
-    for step in range(ITERS):
+    profile_y = jnp.asarray(ones_profile(densities.shape[2]))
+    profile_z = jnp.asarray(ones_profile(densities.shape[3]))
+    blur_ones = profile_x[:, None, None] * profile_y[None, :, None] * profile_z[None, None, :]
+    raw_d = heat_blur(densities / blur_ones[None])
+    dfield = raw_d / mass[:, None, None, None]
+    partial_log = jnp.sum(lam_local[:, None, None, None] * jnp.log(dfield), axis=0)
+    barycenter = jnp.exp(lax.psum(partial_log, "dev"))
+    scal = barycenter[None] / dfield
+    field = densities / mass[:, None, None, None]
+    for step in range(1, ITERS):
         wfield = field / heat_blur(scal)
         dfield = scal * heat_blur(wfield)
         partial_log = jnp.sum(lam_local[:, None, None, None] * jnp.log(dfield), axis=0)
         barycenter = jnp.exp(lax.psum(partial_log, "dev"))
         scal = scal * barycenter[None] / dfield
-        rounds = rounds + 1
     return (barycenter, scal)
 
 

time: 466 us -> 382 us (0.82)
  waiting for transfers between devices: 206 us -> 169 us
  other arithmetic: 119 us -> 84.7 us
  starting transfers between devices: 25.3 us -> 19.4 us
  blocking collectives: 95.7 us -> 90.3 us
    ppermute x4 -> x3, waiting for transfers between devices: 97.3 us -> 65.6 us  [padded_2(): lax.ppermute(head, axis, [((i + 1) % count, i) for i in range(ends)])]
    div x2 -> x1, other arithmetic: 32.2 us -> 11.2 us  [per_device(): wfield = field / heat_blur(scal)]
    add x8 -> x6, other arithmetic: 55.7 us -> 38.8 us  [taps_over(): total + gauss_taps[index] * lax.slice_in_dim(padded, index, index + lengt...]
    psum x1, blocking collectives: 95.7 us -> 90.3 us  [per_device(): mass = lax.psum(local_sums, 'gx') / cells]
    ppermute x4 -> x3, starting transfers between devices: 14.5 us -> 11.4 us  [padded_2(): lax.ppermute(tail, axis, [(i, (i + 1) % count) for i in range(ends)])]
    ppermute x4 -> x3, starting transfers between devices: 10.7 us -> 7.89 us  [padded_2(): lax.ppermute(head, axis, [((i + 1) % count, i) for i in range(ends)])]
  transfers between devices with their start and end apart: 10 -> 8, of which waited for: 8 -> 6; matrix products, arithmetic and copies ran while one was open for 0% -> 0% of each run, Pallas kernels for 0% -> 0%
where the time goes in v1:
time: 382 us
  waiting for transfers between devices  169 us (44%)
  blocking collectives  90.3 us (24%)
  other arithmetic  84.7 us (22%)
  starting transfers between devices  19.4 us (5%)
  between operations  14.2 us (4%)
  local copies, waits for them, and re-layouts  4.34 us (1%)
    psum x2, waiting for transfers between devices, per_device(): barycenter = jnp.exp(lax.psum(partial_log, 'dev'))  101 us
    psum x1, blocking collectives, per_device(): mass = lax.psum(local_sums, 'gx') / cells  90.3 us
    ppermute x3, waiting for transfers between devices, padded_2(): lax.ppermute(head, axis, [((i + 1) % count, i) for i in range(ends)])  65.6 us
    add x6, other arithmetic, taps_over(): total + gauss_taps[index] * lax.slice_in_dim(padded, index, index + lengt...  38.8 us
    reduce_sum x2, other arithmetic, per_device(): jnp.sum(lam_local[:, None, None, None] * jnp.log(dfield), axis=0)  23.5 us
    ppermute x3, starting transfers between devices, padded_2(): lax.ppermute(tail, axis, [(i, (i + 1) % count) for i in range(ends)])  11.4 us
    div x1, other arithmetic, per_device(): wfield = field / heat_blur(scal)  11.2 us
    ppermute x3, starting transfers between devices, padded_2(): lax.ppermute(head, axis, [((i + 1) % count, i) for i in range(ends)])  7.89 us
  transfers between devices with their start and end apart: 8, of which 6 were waited for; matrix products, arithmetic and copies ran while one was open for 0% of the time, Pallas kernels for 0%

profile of v1, /device:TPU:1, one launch (start us, length us, event | category | flops | bytes accessed | tf_op | source)
XLA Modules:
  0.0 382.0 jit_solution(10756393211832544196)
XLA Ops:
  9.7 2.6 broadcast_divide_fusion
  12.3 3.3 collective-permute-start.1
  15.6 3.6 collective-permute-start
  19.2 90.3 %psum.21 = f32[2]{0:T(128)S(1)} all-reduce(f32[2]{0:T(128)S(1)} %get-tuple-element.7), channel_id=1, replica_groups=mesh['gx'=32,'dev'=4] {'gx'}, use_global_device_ids=true, to_apply=%region_2.0 | all-reduce | flops 2 | bytes 16 | tf_op jit(solution)/shard_map/psum | solution.py:78
  110.8 9.5 %fusion.60 = f32[2,6,256,256]{3,2,1,0:T(8,128)S(1)} fusion(f32[2,6,256,256]{3,2,1,0:T(8,128)S(1)} %get-tuple-element.6, f32[2,6,256,256]{3,2,1,0:T(8,128)} %collective-permute-done.1, f32[2,6,256,256]{3,2,1,0:T(8,128)} %collective-permute-done), kind=kLoop, calls=%fused_computation.144 | loop fusion | flops 27525120 | bytes 12582912 | tf_op jit(solution)/shard_map/add | solution.py:34
  120.2 5.0 %multiply_add_fusion.2 = f32[2,6,256,256]{3,2,1,0:T(8,128)S(1)} fusion(f32[2,6,256,256]{3,2,1,0:T(8,128)S(1)} %fusion.60), kind=kLoop, calls=%fused_computation.289 | loop fusion | flops 19660800 | bytes 6291456 | tf_op jit(solution)/shard_map/add | solution.py:34
  125.3 11.3 %multiply_reduce_fusion.1 = (f32[6,256,256]{2,1,0:T(8,128)}, f32[2,6,256,256]{3,2,1,0:T(8,128)S(1)}) fusion(f32[2]{0:T(128)S(1)} %broadcast_multiply_fusion.2, f32[2]{0:T(128)S(1)} %dynamic_slice.6, f32[2,6,256,256]{3,2,1,0:T(8,128)S(1)} %multiply_add_fusion.2), kind=kLoop, calls=%fused_computation.288 | loop fusion | flops 21626880 | bytes 7864336 | tf_op jit(solution)/shard_map/reduce_sum | solution.py:87
  136.6 46.5 %all-reduce.9.cloned.1.call-done = f32[6,256,256]{2,1,0:T(8,128)} async-done(((f32[6,256,256]{2,1,0:T(8,128)}), f32[6,256,256]{2,1,0:T(8,128)}) %all-reduce.9.cloned.1.call-update) | async-done | bytes 1572880 | tf_op jit(solution)/shard_map/psum | solution.py:88
  183.1 1.6 exp.6
  185.4 2.7 collective-permute-start.3
  188.1 3.3 collective-permute-start.2
  191.4 32.8 %collective-permute-done.3 = f32[2,6,256,256]{3,2,1,0:T(8,128)S(1)} collective-permute-done((f32[2,6,256,256]{3,2,1,0:T(8,128)S(1)}, f32[2,6,256,256]{3,2,1,0:T(8,128)S(1)}, u32[]{:S(2)}, u32[]{:S(2)}) %collective-permute-start.3) | collective-permute-done | bytes 3145760 | tf_op jit(solution)/shard_map/ppermute | solution.py:24
  225.4 4.6 %fusion.32 = f32[2,6,256,256]{3,2,1,0:T(8,128)S(1)} fusion(f32[2,6,256,256]{3,2,1,0:T(8,128)S(1)} %multiply_divide_fusion.1, f32[2,6,256,256]{3,2,1,0:T(8,128)S(1)} %collective-permute-done.3, f32[2,6,256,256]{3,2,1,0:T(8,128)S(1)} %collective-permute-done.2), kind=kLoop, calls=%fused_computation.116 | loop fusion | flops 27525120 | bytes 12582912 | tf_op jit(solution)/shard_map/add | solution.py:34
  230.0 5.0 %multiply_add_fusion.1 = f32[2,6,256,256]{3,2,1,0:T(8,128)S(1)} fusion(f32[2,6,256,256]{3,2,1,0:T(8,128)S(1)} %fusion.32), kind=kLoop, calls=%fused_computation.272 | loop fusion | flops 19660800 | bytes 6291456 | tf_op jit(solution)/shard_map/add | solution.py:34
  235.0 11.2 %fusion.122 = f32[2,6,256,256]{3,2,1,0:T(8,128)S(1)} fusion(f32[2,6,256,256]{3,2,1,0:T(8,128)} %param.5, f32[2,6,256,256]{3,2,1,0:T(8,128)S(1)} %multiply_add_fusion.1, f32[2]{0:T(128)S(1)} %broadcast_multiply_fusion.2), kind=kLoop, calls=%fused_computation.206 | loop fusion | flops 21233664 | bytes 9437192 | tf_op jit(solution)/shard_map/div | solution.py:92
  246.3 1.9 collective-permute-start.5
  248.2 4.6 %collective-permute-start.4 = (f32[2,6,256,256]{3,2,1,0:T(8,128)S(1)}, f32[2,6,256,256]{3,2,1,0:T(8,128)S(1)}, u32[]{:S(2)}, u32[]{:S(2)}) collective-permute-start(f32[2,6,256,256]{3,2,1,0:T(8,128)S(1)} %fusion.122), channel_id=1, source_target_pairs={{0,4},{4,8},{8,12},{12,16},{16,20},{20,24},{24,28},{28,32},{32,36}... | collective-permute-start | bytes 9437192 | tf_op jit(solution)/shard_map/ppermute | solution.py:22
  252.8 32.8 %collective-permute-done.5 = f32[2,6,256,256]{3,2,1,0:T(8,128)S(1)} collective-permute-done((f32[2,6,256,256]{3,2,1,0:T(8,128)S(1)}, f32[2,6,256,256]{3,2,1,0:T(8,128)S(1)}, u32[]{:S(2)}, u32[]{:S(2)}) %collective-permute-start.5) | collective-permute-done | bytes 3145760 | tf_op jit(solution)/shard_map/ppermute | solution.py:24
  286.8 9.7 %fusion.4 = f32[2,6,256,256]{3,2,1,0:T(8,128)S(1)} fusion(f32[2,6,256,256]{3,2,1,0:T(8,128)} %copy-done.2, f32[2,6,256,256]{3,2,1,0:T(8,128)S(1)} %collective-permute-done.5, f32[2,6,256,256]{3,2,1,0:T(8,128)S(1)} %collective-permute-done.4), kind=kLoop, calls=%fused_computation.88 | loop fusion | flops 27525120 | bytes 12582912 | tf_op jit(solution)/shard_map/add | solution.py:34
  296.5 5.0 %multiply_add_fusion = f32[2,6,256,256]{3,2,1,0:T(8,128)S(1)} fusion(f32[2,6,256,256]{3,2,1,0:T(8,128)S(1)} %fusion.4), kind=kLoop, calls=%fused_computation.257 | loop fusion | flops 19660800 | bytes 6291456 | tf_op jit(solution)/shard_map/add | solution.py:34
  301.6 12.2 %multiply_reduce_fusion = (f32[6,256,256]{2,1,0:T(8,128)}, f32[2,6,256,256]{3,2,1,0:T(8,128)}) fusion(f32[2]{0:T(128)S(1)} %dynamic_slice.6, f32[2,6,256,256]{3,2,1,0:T(8,128)S(1)} %multiply_add_fusion, f32[2,6,256,256]{3,2,1,0:T(8,128)S(1)} %get-tuple-element.5, f32[2]{0:T(128)S(1)} %broadcast_multiply_fusion.2, f32[6,256,256]{2,1,0:T(8,128)S(1)} %exp.6), kind=kLoop, calls=%fused_computation.256 | loop fusion | flops 23199744 | bytes 12582928 | tf_op jit(solution)/shard_map/reduce_sum | solution.py:94
  313.8 54.6 %all-reduce.11.cloned.1.call-done = f32[6,256,256]{2,1,0:T(8,128)} async-done(((f32[6,256,256]{2,1,0:T(8,128)}), f32[6,256,256]{2,1,0:T(8,128)}) %all-reduce.11.cloned.1.call-update) | async-done | bytes 1572880 | tf_op jit(solution)/shard_map/psum | solution.py:95
  368.4 1.7 exp.7
  370.3 4.9 %multiply_divide_fusion = f32[2,6,256,256]{3,2,1,0:T(8,128)} fusion(f32[2,6,256,256]{3,2,1,0:T(8,128)} %get-tuple-element.3, f32[6,256,256]{2,1,0:T(8,128)S(1)} %exp.7, f32[2,6,256,256]{3,2,1,0:T(8,128)S(1)} %get-tuple-element.5, f32[2]{0:T(128)S(1)} %broadcast_multiply_fusion.2, f32[6,256,256]{2,1,0:T(8,128)S(1)} %copy-done.1), kind=kLoop, calls=%fused_computation.255 | loop fusion | flops 3145728 | bytes 12582920 | tf_op jit(solution)/shard_map/div | solution.py:96
  (26 shorter events, 7.1 us)
Async XLA Ops:
  7.2 176.0 %all-reduce.9.cloned.1.call-start = ((), (), s32[]{:S(2)}) async-start(), calls=%async_computation | async-start | bytes 3145728 | tf_op jit(solution)/shard_map/psum | solution.py:88
  9.7 99.8 %copy-start.4 = (f32[8]{0:T(128)S(1)}, f32[8]{0:T(128)}, u32[]{:S(2)}) copy-start(f32[8]{0:T(128)} %param.6) | copy-start | bytes 100
  12.3 98.5 %collective-permute-start.1 = (f32[2,6,256,256]{3,2,1,0:T(8,128)S(1)}, f32[2,6,256,256]{3,2,1,0:T(8,128)}, u32[]{:S(2)}, u32[]{:S(2)}) collective-permute-start(f32[2,6,256,256]{3,2,1,0:T(8,128)S(1)} %get-tuple-element.6), channel_id=1, source_target_pairs={{4,0},{8,4},{12,8},{16,12},{20,16},{24,20},{28,24},{32,28},{36,32}... | collective-permute-start | bytes 9437192 | tf_op jit(solution)/shard_map/ppermute | solution.py:24
  15.6 95.2 %collective-permute-start = (f32[2,6,256,256]{3,2,1,0:T(8,128)S(1)}, f32[2,6,256,256]{3,2,1,0:T(8,128)}, u32[]{:S(2)}, u32[]{:S(2)}) collective-permute-start(f32[2,6,256,256]{3,2,1,0:T(8,128)S(1)} %get-tuple-element.6), channel_id=1, source_target_pairs={{0,4},{4,8},{8,12},{12,16},{16,20},{20,24},{24,28},{28,32},{32,36}... | collective-permute-start | bytes 9437192 | tf_op jit(solution)/shard_map/ppermute | solution.py:22
  136.6 231.8 %all-reduce.11.cloned.1.call-start = ((), (), s32[]{:S(2)}) async-start(), calls=%async_computation.1 | async-start | bytes 3145728 | tf_op jit(solution)/shard_map/psum | solution.py:95
  184.7 116.8 %copy-start = (f32[6,256,256]{2,1,0:T(8,128)}, f32[6,256,256]{2,1,0:T(8,128)S(1)}, u32[]{:S(2)}) copy-start(f32[6,256,256]{2,1,0:T(8,128)S(1)} %exp.6) | copy-start | bytes 4718596
  185.4 38.8 %collective-permute-start.3 = (f32[2,6,256,256]{3,2,1,0:T(8,128)S(1)}, f32[2,6,256,256]{3,2,1,0:T(8,128)S(1)}, u32[]{:S(2)}, u32[]{:S(2)}) collective-permute-start(f32[2,6,256,256]{3,2,1,0:T(8,128)S(1)} %multiply_divide_fusion.1), channel_id=1, source_target_pairs={{4,0},{8,4},{12,8},{16,12},{20,16},{24,20},{28,24},{32,28},{36,32}... | collective-permute-start | bytes 9437192 | tf_op jit(solution)/shard_map/ppermute | solution.py:24
  188.1 37.3 %collective-permute-start.2 = (f32[2,6,256,256]{3,2,1,0:T(8,128)S(1)}, f32[2,6,256,256]{3,2,1,0:T(8,128)S(1)}, u32[]{:S(2)}, u32[]{:S(2)}) collective-permute-start(f32[2,6,256,256]{3,2,1,0:T(8,128)S(1)} %multiply_divide_fusion.1), channel_id=1, source_target_pairs={{0,4},{4,8},{8,12},{12,16},{16,20},{20,24},{24,28},{28,32},{32,36}... | collective-permute-start | bytes 9437192 | tf_op jit(solution)/shard_map/ppermute | solution.py:22
  246.2 39.4 %copy-start.2 = (f32[2,6,256,256]{3,2,1,0:T(8,128)}, f32[2,6,256,256]{3,2,1,0:T(8,128)S(1)}, u32[]{:S(2)}) copy-start(f32[2,6,256,256]{3,2,1,0:T(8,128)S(1)} %fusion.122) | copy-start | bytes 9437188
  246.3 39.3 %collective-permute-start.5 = (f32[2,6,256,256]{3,2,1,0:T(8,128)S(1)}, f32[2,6,256,256]{3,2,1,0:T(8,128)S(1)}, u32[]{:S(2)}, u32[]{:S(2)}) collective-permute-start(f32[2,6,256,256]{3,2,1,0:T(8,128)S(1)} %fusion.122), channel_id=1, source_target_pairs={{4,0},{8,4},{12,8},{16,12},{20,16},{24,20},{28,24},{32,28},{36,32}... | collective-permute-start | bytes 9437192 | tf_op jit(solution)/shard_map/ppermute | solution.py:24
  248.2 38.6 %collective-permute-start.4 = (f32[2,6,256,256]{3,2,1,0:T(8,128)S(1)}, f32[2,6,256,256]{3,2,1,0:T(8,128)S(1)}, u32[]{:S(2)}, u32[]{:S(2)}) collective-permute-start(f32[2,6,256,256]{3,2,1,0:T(8,128)S(1)} %fusion.122), channel_id=1, source_target_pairs={{0,4},{4,8},{8,12},{12,16},{16,20},{20,24},{24,28},{28,32},{32,36}... | collective-permute-start | bytes 9437192 | tf_op jit(solution)/shard_map/ppermute | solution.py:22
  368.4 1.9 copy-start.1
  370.2 5.0 %copy-start.3 = (f32[6,256,256]{2,1,0:T(8,128)}, f32[6,256,256]{2,1,0:T(8,128)S(1)}, u32[]{:S(2)}) copy-start(f32[6,256,256]{2,1,0:T(8,128)S(1)} %exp.7) | copy-start | bytes 4718596
Sparse Core Ops, SparseCore 0:
  136.7 46.3 all-reduce.8
  313.9 54.4 all-reduce.10

commit v2 on v1

--- a/solution.py
+++ b/solution.py
@@ -75,7 +75,7 @@
     total_planes = planes * lax.axis_size("gx")
     cells = total_planes * densities.shape[2] * densities.shape[3]
     local_sums = jnp.sum(densities, axis=(1, 2, 3))
-    mass = lax.psum(local_sums, "gx") / cells
+    mass = lax.psum(jnp.broadcast_to(local_sums[:, None], (local_sums.shape[0], 8192)), "gx")[:, 0] / cells
     profile_x = lax.dynamic_slice_in_dim(
         jnp.asarray(ones_profile(total_planes)), lax.axis_index("gx") * planes, planes
     )

time: 382 us -> 423 us (1.11)
  waiting for transfers between devices: 169 us -> 297 us
  blocking collectives: 90.3 us -> 0 us
    psum x0 -> x1, waiting for transfers between devices: none -> 124 us  [per_device(): lax.psum(jnp.broadcast_to(local_sums[:, None], (local_sums.shape[0], 8192...]
    psum x1 -> x0, blocking collectives: 90.3 us -> none  [per_device(): mass = lax.psum(local_sums, 'gx') / cells]
  transfers between devices with their start and end apart: 8 -> 9, of which waited for: 6 -> 7; matrix products, arithmetic and copies ran while one was open for 0% -> 1% of each run, Pallas kernels for 0% -> 0%
where the time goes in v2:
time: 423 us; the launch traced here: 422 us
  waiting for transfers between devices  297 us (70%)
  other arithmetic  85.1 us (20%)
  starting transfers between devices  19.4 us (5%)
  between operations  13.9 us (3%)
  local copies, waits for them, and re-layouts  7.16 us (2%)
    psum x1, waiting for transfers between devices, per_device(): lax.psum(jnp.broadcast_to(local_sums[:, None], (local_sums.shape[0], 8192...  124 us
    psum x2, waiting for transfers between devices, per_device(): barycenter = jnp.exp(lax.psum(partial_log, 'dev'))  105 us
    ppermute x3, waiting for transfers between devices, padded_2(): lax.ppermute(head, axis, [((i + 1) % count, i) for i in range(ends)])  65.6 us
    add x6, other arithmetic, taps_over(): total + gauss_taps[index] * lax.slice_in_dim(padded, index, index + lengt...  38.7 us
    reduce_sum x2, other arithmetic, per_device(): jnp.sum(lam_local[:, None, None, None] * jnp.log(dfield), axis=0)  23.5 us
    ppermute x3, starting transfers between devices, padded_2(): lax.ppermute(tail, axis, [(i, (i + 1) % count) for i in range(ends)])  11.4 us
    div x1, other arithmetic, per_device(): wfield = field / heat_blur(scal)  11.2 us
  transfers between devices with their start and end apart: 9, of which 7 were waited for; matrix products, arithmetic and copies ran while one was open for 1% of the time, Pallas kernels for 0%

profile of v2, /device:TPU:1, one launch (start us, length us, event | category | flops | bytes accessed | tf_op | source)
XLA Modules:
  0.0 422.2 jit_solution(13211919444642104156)
XLA Ops:
  9.7 2.6 broadcast_divide_fusion
  12.3 3.3 collective-permute-start.1
  15.6 3.6 collective-permute-start
  19.1 2.2 broadcast_in_dim.2
  23.4 123.9 %all-reduce.10.cloned.1.call-done = f32[2,8192]{0,1:T(8,128)} async-done(((f32[2,8192]{0,1:T(8,128)}), f32[2,8192]{0,1:T(8,128)}) %all-reduce.10.cloned.1.call-update) | async-done | bytes 65552 | tf_op jit(solution)/shard_map/psum | solution.py:78
  147.9 9.5 %fusion.60 = f32[2,6,256,256]{3,2,1,0:T(8,128)S(1)} fusion(f32[2,6,256,256]{3,2,1,0:T(8,128)S(1)} %get-tuple-element.6, f32[2,6,256,256]{3,2,1,0:T(8,128)} %collective-permute-done.1, f32[2,6,256,256]{3,2,1,0:T(8,128)} %collective-permute-done), kind=kLoop, calls=%fused_computation.144 | loop fusion | flops 27525120 | bytes 12582912 | tf_op jit(solution)/shard_map/add | solution.py:34
  157.4 5.0 %multiply_add_fusion.2 = f32[2,6,256,256]{3,2,1,0:T(8,128)S(1)} fusion(f32[2,6,256,256]{3,2,1,0:T(8,128)S(1)} %fusion.60), kind=kLoop, calls=%fused_computation.289 | loop fusion | flops 19660800 | bytes 6291456 | tf_op jit(solution)/shard_map/add | solution.py:34
  162.5 11.3 %multiply_reduce_fusion.1 = (f32[6,256,256]{2,1,0:T(8,128)}, f32[2,6,256,256]{3,2,1,0:T(8,128)S(1)}) fusion(f32[2]{0:T(128)S(1)} %fusion.192, f32[2]{0:T(128)S(1)} %dynamic_slice.6, f32[2,6,256,256]{3,2,1,0:T(8,128)S(1)} %multiply_add_fusion.2), kind=kLoop, calls=%fused_computation.288 | loop fusion | flops 21626880 | bytes 7864336 | tf_op jit(solution)/shard_map/reduce_sum | solution.py:87
  173.8 50.0 %all-reduce.12.cloned.1.call-done = f32[6,256,256]{2,1,0:T(8,128)} async-done(((f32[6,256,256]{2,1,0:T(8,128)}), f32[6,256,256]{2,1,0:T(8,128)}) %all-reduce.12.cloned.1.call-update) | async-done | bytes 1572880 | tf_op jit(solution)/shard_map/psum | solution.py:88
  226.2 2.7 collective-permute-start.3
  228.8 3.3 collective-permute-start.2
  232.1 32.8 %collective-permute-done.3 = f32[2,6,256,256]{3,2,1,0:T(8,128)S(1)} collective-permute-done((f32[2,6,256,256]{3,2,1,0:T(8,128)S(1)}, f32[2,6,256,256]{3,2,1,0:T(8,128)S(1)}, u32[]{:S(2)}, u32[]{:S(2)}) %collective-permute-start.3) | collective-permute-done | bytes 3145760 | tf_op jit(solution)/shard_map/ppermute | solution.py:24
  266.1 4.6 %fusion.32 = f32[2,6,256,256]{3,2,1,0:T(8,128)S(1)} fusion(f32[2,6,256,256]{3,2,1,0:T(8,128)S(1)} %multiply_divide_fusion.1, f32[2,6,256,256]{3,2,1,0:T(8,128)S(1)} %collective-permute-done.3, f32[2,6,256,256]{3,2,1,0:T(8,128)S(1)} %collective-permute-done.2), kind=kLoop, calls=%fused_computation.116 | loop fusion | flops 27525120 | bytes 12582912 | tf_op jit(solution)/shard_map/add | solution.py:34
  270.7 5.0 %multiply_add_fusion.1 = f32[2,6,256,256]{3,2,1,0:T(8,128)S(1)} fusion(f32[2,6,256,256]{3,2,1,0:T(8,128)S(1)} %fusion.32), kind=kLoop, calls=%fused_computation.272 | loop fusion | flops 19660800 | bytes 6291456 | tf_op jit(solution)/shard_map/add | solution.py:34
  275.7 11.2 %fusion.122 = f32[2,6,256,256]{3,2,1,0:T(8,128)S(1)} fusion(f32[2,6,256,256]{3,2,1,0:T(8,128)} %param.5, f32[2,6,256,256]{3,2,1,0:T(8,128)S(1)} %multiply_add_fusion.1, f32[2]{0:T(128)S(1)} %fusion.192), kind=kLoop, calls=%fused_computation.206 | loop fusion | flops 21233664 | bytes 9437192 | tf_op jit(solution)/shard_map/div | solution.py:92
  287.0 1.9 collective-permute-start.5
  288.9 4.6 %collective-permute-start.4 = (f32[2,6,256,256]{3,2,1,0:T(8,128)S(1)}, f32[2,6,256,256]{3,2,1,0:T(8,128)S(1)}, u32[]{:S(2)}, u32[]{:S(2)}) collective-permute-start(f32[2,6,256,256]{3,2,1,0:T(8,128)S(1)} %fusion.122), channel_id=1, source_target_pairs={{0,4},{4,8},{8,12},{12,16},{16,20},{20,24},{24,28},{28,32},{32,36}... | collective-permute-start | bytes 9437192 | tf_op jit(solution)/shard_map/ppermute | solution.py:22
  293.5 32.8 %collective-permute-done.5 = f32[2,6,256,256]{3,2,1,0:T(8,128)S(1)} collective-permute-done((f32[2,6,256,256]{3,2,1,0:T(8,128)S(1)}, f32[2,6,256,256]{3,2,1,0:T(8,128)S(1)}, u32[]{:S(2)}, u32[]{:S(2)}) %collective-permute-start.5) | collective-permute-done | bytes 3145760 | tf_op jit(solution)/shard_map/ppermute | solution.py:24
  327.5 9.5 %fusion.4 = f32[2,6,256,256]{3,2,1,0:T(8,128)S(1)} fusion(f32[2,6,256,256]{3,2,1,0:T(8,128)} %copy-done.2, f32[2,6,256,256]{3,2,1,0:T(8,128)S(1)} %collective-permute-done.5, f32[2,6,256,256]{3,2,1,0:T(8,128)S(1)} %collective-permute-done.4), kind=kLoop, calls=%fused_computation.88 | loop fusion | flops 27525120 | bytes 12582912 | tf_op jit(solution)/shard_map/add | solution.py:34
  337.1 5.0 %multiply_add_fusion = f32[2,6,256,256]{3,2,1,0:T(8,128)S(1)} fusion(f32[2,6,256,256]{3,2,1,0:T(8,128)S(1)} %fusion.4), kind=kLoop, calls=%fused_computation.257 | loop fusion | flops 19660800 | bytes 6291456 | tf_op jit(solution)/shard_map/add | solution.py:34
  342.1 12.2 %multiply_reduce_fusion = (f32[6,256,256]{2,1,0:T(8,128)}, f32[2,6,256,256]{3,2,1,0:T(8,128)}) fusion(f32[2]{0:T(128)S(1)} %dynamic_slice.6, f32[2,6,256,256]{3,2,1,0:T(8,128)S(1)} %multiply_add_fusion, f32[2,6,256,256]{3,2,1,0:T(8,128)S(1)} %get-tuple-element.5, f32[2]{0:T(128)S(1)} %fusion.192, f32[6,256,256]{2,1,0:T(8,128)S(1)} %exp.6), kind=kLoop, calls=%fused_computation.256 | loop fusion | flops 23199744 | bytes 12582928 | tf_op jit(solution)/shard_map/reduce_sum | solution.py:94
  354.3 54.6 %all-reduce.14.cloned.1.call-done = f32[6,256,256]{2,1,0:T(8,128)} async-done(((f32[6,256,256]{2,1,0:T(8,128)}), f32[6,256,256]{2,1,0:T(8,128)}) %all-reduce.14.cloned.1.call-update) | async-done | bytes 1572880 | tf_op jit(solution)/shard_map/psum | solution.py:95
  409.0 1.7 exp.7
  410.8 4.9 %multiply_divide_fusion = f32[2,6,256,256]{3,2,1,0:T(8,128)} fusion(f32[2,6,256,256]{3,2,1,0:T(8,128)} %get-tuple-element.3, f32[6,256,256]{2,1,0:T(8,128)S(1)} %exp.7, f32[2,6,256,256]{3,2,1,0:T(8,128)S(1)} %get-tuple-element.5, f32[2]{0:T(128)S(1)} %fusion.192, f32[6,256,256]{2,1,0:T(8,128)S(1)} %copy-done.1), kind=kLoop, calls=%fused_computation.255 | loop fusion | flops 3145728 | bytes 12582920 | tf_op jit(solution)/shard_map/div | solution.py:96
  (29 shorter events, 10.0 us)
Async XLA Ops:
  7.2 140.1 %all-reduce.10.cloned.1.call-start = ((), (), s32[]{:S(2)}) async-start(), calls=%async_computation | async-start | bytes 8388608 | tf_op jit(solution)/shard_map/psum | solution.py:78
  12.3 135.7 %collective-permute-start.1 = (f32[2,6,256,256]{3,2,1,0:T(8,128)S(1)}, f32[2,6,256,256]{3,2,1,0:T(8,128)}, u32[]{:S(2)}, u32[]{:S(2)}) collective-permute-start(f32[2,6,256,256]{3,2,1,0:T(8,128)S(1)} %get-tuple-element.6), channel_id=1, source_target_pairs={{4,0},{8,4},{12,8},{16,12},{20,16},{24,20},{28,24},{32,28},{36,32}... | collective-permute-start | bytes 9437192 | tf_op jit(solution)/shard_map/ppermute | solution.py:24
  15.6 132.4 %collective-permute-start = (f32[2,6,256,256]{3,2,1,0:T(8,128)S(1)}, f32[2,6,256,256]{3,2,1,0:T(8,128)}, u32[]{:S(2)}, u32[]{:S(2)}) collective-permute-start(f32[2,6,256,256]{3,2,1,0:T(8,128)S(1)} %get-tuple-element.6), channel_id=1, source_target_pairs={{0,4},{4,8},{8,12},{12,16},{16,20},{20,24},{24,28},{28,32},{32,36}... | collective-permute-start | bytes 9437192 | tf_op jit(solution)/shard_map/ppermute | solution.py:22
  21.4 0.7 copy-start.4
  21.4 202.4 %all-reduce.12.cloned.1.call-start = ((), (), s32[]{:S(2)}) async-start(), calls=%async_computation.1 | async-start | bytes 3145728 | tf_op jit(solution)/shard_map/psum | solution.py:88
  173.8 235.2 %all-reduce.14.cloned.1.call-start = ((), (), s32[]{:S(2)}) async-start(), calls=%async_computation.2 | async-start | bytes 3145728 | tf_op jit(solution)/shard_map/psum | solution.py:95
  225.5 116.6 %copy-start = (f32[6,256,256]{2,1,0:T(8,128)}, f32[6,256,256]{2,1,0:T(8,128)S(1)}, u32[]{:S(2)}) copy-start(f32[6,256,256]{2,1,0:T(8,128)S(1)} %exp.6) | copy-start | bytes 4718596
  226.2 38.8 %collective-permute-start.3 = (f32[2,6,256,256]{3,2,1,0:T(8,128)S(1)}, f32[2,6,256,256]{3,2,1,0:T(8,128)S(1)}, u32[]{:S(2)}, u32[]{:S(2)}) collective-permute-start(f32[2,6,256,256]{3,2,1,0:T(8,128)S(1)} %multiply_divide_fusion.1), channel_id=1, source_target_pairs={{4,0},{8,4},{12,8},{16,12},{20,16},{24,20},{28,24},{32,28},{36,32}... | collective-permute-start | bytes 9437192 | tf_op jit(solution)/shard_map/ppermute | solution.py:24
  228.8 37.3 %collective-permute-start.2 = (f32[2,6,256,256]{3,2,1,0:T(8,128)S(1)}, f32[2,6,256,256]{3,2,1,0:T(8,128)S(1)}, u32[]{:S(2)}, u32[]{:S(2)}) collective-permute-start(f32[2,6,256,256]{3,2,1,0:T(8,128)S(1)} %multiply_divide_fusion.1), channel_id=1, source_target_pairs={{0,4},{4,8},{8,12},{12,16},{16,20},{20,24},{24,28},{28,32},{32,36}... | collective-permute-start | bytes 9437192 | tf_op jit(solution)/shard_map/ppermute | solution.py:22
  287.0 39.4 %copy-start.2 = (f32[2,6,256,256]{3,2,1,0:T(8,128)}, f32[2,6,256,256]{3,2,1,0:T(8,128)S(1)}, u32[]{:S(2)}) copy-start(f32[2,6,256,256]{3,2,1,0:T(8,128)S(1)} %fusion.122) | copy-start | bytes 9437188
  287.0 39.3 %collective-permute-start.5 = (f32[2,6,256,256]{3,2,1,0:T(8,128)S(1)}, f32[2,6,256,256]{3,2,1,0:T(8,128)S(1)}, u32[]{:S(2)}, u32[]{:S(2)}) collective-permute-start(f32[2,6,256,256]{3,2,1,0:T(8,128)S(1)} %fusion.122), channel_id=1, source_target_pairs={{4,0},{8,4},{12,8},{16,12},{20,16},{24,20},{28,24},{32,28},{36,32}... | collective-permute-start | bytes 9437192 | tf_op jit(solution)/shard_map/ppermute | solution.py:24
  288.9 38.6 %collective-permute-start.4 = (f32[2,6,256,256]{3,2,1,0:T(8,128)S(1)}, f32[2,6,256,256]{3,2,1,0:T(8,128)S(1)}, u32[]{:S(2)}, u32[]{:S(2)}) collective-permute-start(f32[2,6,256,256]{3,2,1,0:T(8,128)S(1)} %fusion.122), channel_id=1, source_target_pairs={{0,4},{4,8},{8,12},{12,16},{16,20},{20,24},{24,28},{28,32},{32,36}... | collective-permute-start | bytes 9437192 | tf_op jit(solution)/shard_map/ppermute | solution.py:22
  408.9 1.9 copy-start.1
  410.7 5.0 %copy-start.3 = (f32[6,256,256]{2,1,0:T(8,128)}, f32[6,256,256]{2,1,0:T(8,128)S(1)}, u32[]{:S(2)}) copy-start(f32[6,256,256]{2,1,0:T(8,128)S(1)} %exp.7) | copy-start | bytes 4718596
Sparse Core Ops, SparseCore 0:
  21.5 125.6 all-reduce.9
  173.9 49.8 all-reduce.11
  354.4 54.4 all-reduce.13

commit v3 on v2

--- a/solution.py
+++ b/solution.py
@@ -75,7 +75,7 @@
     total_planes = planes * lax.axis_size("gx")
     cells = total_planes * densities.shape[2] * densities.shape[3]
     local_sums = jnp.sum(densities, axis=(1, 2, 3))
-    mass = lax.psum(jnp.broadcast_to(local_sums[:, None], (local_sums.shape[0], 8192)), "gx")[:, 0] / cells
+    mass = jnp.sum(lax.all_gather(local_sums, "gx"), axis=0) / cells
     profile_x = lax.dynamic_slice_in_dim(
         jnp.asarray(ones_profile(total_planes)), lax.axis_index("gx") * planes, planes
     )

time: 423 us -> 382 us (0.903)
  waiting for transfers between devices: 297 us -> 169 us
  blocking collectives: 0 us -> 88.2 us
    psum x1 -> x0, waiting for transfers between devices: 124 us -> none  [per_device(): lax.psum(jnp.broadcast_to(local_sums[:, None], (local_sums.shape[0], 8192...]
    unnamed x0 -> x1, blocking collectives: none -> 88.2 us
  transfers between devices with their start and end apart: 9 -> 8, of which waited for: 7 -> 6; matrix products, arithmetic and copies ran while one was open for 1% -> 1% of each run, Pallas kernels for 0% -> 0%
where the time goes in v3:
time: 382 us
  waiting for transfers between devices  169 us (44%)
  blocking collectives  88.2 us (23%)
  other arithmetic  84.7 us (22%)
  starting transfers between devices  19.4 us (5%)
  between operations  14.9 us (4%)
  local copies, waits for them, and re-layouts  5.27 us (1%)
    psum x2, waiting for transfers between devices, per_device(): barycenter = jnp.exp(lax.psum(partial_log, 'dev'))  101 us
    unnamed x1, blocking collectives  88.2 us
    ppermute x3, waiting for transfers between devices, padded_2(): lax.ppermute(head, axis, [((i + 1) % count, i) for i in range(ends)])  65.6 us
    add x6, other arithmetic, taps_over(): total + gauss_taps[index] * lax.slice_in_dim(padded, index, index + lengt...  38.8 us
    reduce_sum x2, other arithmetic, per_device(): jnp.sum(lam_local[:, None, None, None] * jnp.log(dfield), axis=0)  23.5 us
    ppermute x3, starting transfers between devices, padded_2(): lax.ppermute(tail, axis, [(i, (i + 1) % count) for i in range(ends)])  11.4 us
    div x1, other arithmetic, per_device(): wfield = field / heat_blur(scal)  11.2 us
    ppermute x3, starting transfers between devices, padded_2(): lax.ppermute(head, axis, [((i + 1) % count, i) for i in range(ends)])  7.89 us
  transfers between devices with their start and end apart: 8, of which 6 were waited for; matrix products, arithmetic and copies ran while one was open for 1% of the time, Pallas kernels for 0%

profile of v3, /device:TPU:1, one launch (start us, length us, event | category | flops | bytes accessed | tf_op | source)
XLA Modules:
  0.0 381.6 jit_solution(14022225569266385720)
XLA Ops:
  9.7 2.6 broadcast_divide_fusion
  12.3 3.3 collective-permute-start.1
  15.6 3.6 collective-permute-start
  21.3 88.2 %all-reduce.6 = f32[64]{0:T(128)S(1)} all-reduce(f32[64]{0:T(128)S(1)} %dynamic-update-slice), channel_id=2, replica_groups=mesh['gx'=32,'dev'=4] {'gx'}, use_global_device_ids=true, to_apply=%add.6 | all-reduce | flops 64 | bytes 512
  110.3 9.5 %fusion.60 = f32[2,6,256,256]{3,2,1,0:T(8,128)S(1)} fusion(f32[2,6,256,256]{3,2,1,0:T(8,128)S(1)} %get-tuple-element.6, f32[2,6,256,256]{3,2,1,0:T(8,128)} %collective-permute-done.1, f32[2,6,256,256]{3,2,1,0:T(8,128)} %collective-permute-done), kind=kLoop, calls=%fused_computation.144 | loop fusion | flops 27525120 | bytes 12582912 | tf_op jit(solution)/shard_map/add | solution.py:34
  119.8 5.0 %multiply_add_fusion.2 = f32[2,6,256,256]{3,2,1,0:T(8,128)S(1)} fusion(f32[2,6,256,256]{3,2,1,0:T(8,128)S(1)} %fusion.60), kind=kLoop, calls=%fused_computation.289 | loop fusion | flops 19660800 | bytes 6291456 | tf_op jit(solution)/shard_map/add | solution.py:34
  124.8 11.3 %multiply_reduce_fusion.1 = (f32[6,256,256]{2,1,0:T(8,128)}, f32[2,6,256,256]{3,2,1,0:T(8,128)S(1)}) fusion(f32[2]{0:T(128)S(1)} %broadcast_multiply_fusion.2, f32[2]{0:T(128)S(1)} %dynamic_slice.6, f32[2,6,256,256]{3,2,1,0:T(8,128)S(1)} %multiply_add_fusion.2), kind=kLoop, calls=%fused_computation.288 | loop fusion | flops 21626880 | bytes 7864336 | tf_op jit(solution)/shard_map/reduce_sum | solution.py:87
  136.2 46.5 %all-reduce.10.cloned.1.call-done = f32[6,256,256]{2,1,0:T(8,128)} async-done(((f32[6,256,256]{2,1,0:T(8,128)}), f32[6,256,256]{2,1,0:T(8,128)}) %all-reduce.10.cloned.1.call-update) | async-done | bytes 1572880 | tf_op jit(solution)/shard_map/psum | solution.py:88
  182.7 1.6 exp.6
  185.0 2.7 collective-permute-start.3
  187.7 3.3 collective-permute-start.2
  190.9 32.8 %collective-permute-done.3 = f32[2,6,256,256]{3,2,1,0:T(8,128)S(1)} collective-permute-done((f32[2,6,256,256]{3,2,1,0:T(8,128)S(1)}, f32[2,6,256,256]{3,2,1,0:T(8,128)S(1)}, u32[]{:S(2)}, u32[]{:S(2)}) %collective-permute-start.3) | collective-permute-done | bytes 3145760 | tf_op jit(solution)/shard_map/ppermute | solution.py:24
  225.0 4.6 %fusion.32 = f32[2,6,256,256]{3,2,1,0:T(8,128)S(1)} fusion(f32[2,6,256,256]{3,2,1,0:T(8,128)S(1)} %multiply_divide_fusion.1, f32[2,6,256,256]{3,2,1,0:T(8,128)S(1)} %collective-permute-done.3, f32[2,6,256,256]{3,2,1,0:T(8,128)S(1)} %collective-permute-done.2), kind=kLoop, calls=%fused_computation.116 | loop fusion | flops 27525120 | bytes 12582912 | tf_op jit(solution)/shard_map/add | solution.py:34
  229.5 5.0 %multiply_add_fusion.1 = f32[2,6,256,256]{3,2,1,0:T(8,128)S(1)} fusion(f32[2,6,256,256]{3,2,1,0:T(8,128)S(1)} %fusion.32), kind=kLoop, calls=%fused_computation.272 | loop fusion | flops 19660800 | bytes 6291456 | tf_op jit(solution)/shard_map/add | solution.py:34
  234.6 11.2 %fusion.122 = f32[2,6,256,256]{3,2,1,0:T(8,128)S(1)} fusion(f32[2,6,256,256]{3,2,1,0:T(8,128)} %param.5, f32[2,6,256,256]{3,2,1,0:T(8,128)S(1)} %multiply_add_fusion.1, f32[2]{0:T(128)S(1)} %broadcast_multiply_fusion.2), kind=kLoop, calls=%fused_computation.206 | loop fusion | flops 21233664 | bytes 9437192 | tf_op jit(solution)/shard_map/div | solution.py:92
  245.8 1.9 collective-permute-start.5
  247.7 4.6 %collective-permute-start.4 = (f32[2,6,256,256]{3,2,1,0:T(8,128)S(1)}, f32[2,6,256,256]{3,2,1,0:T(8,128)S(1)}, u32[]{:S(2)}, u32[]{:S(2)}) collective-permute-start(f32[2,6,256,256]{3,2,1,0:T(8,128)S(1)} %fusion.122), channel_id=1, source_target_pairs={{0,4},{4,8},{8,12},{12,16},{16,20},{20,24},{24,28},{28,32},{32,36}... | collective-permute-start | bytes 9437192 | tf_op jit(solution)/shard_map/ppermute | solution.py:22
  252.4 32.8 %collective-permute-done.5 = f32[2,6,256,256]{3,2,1,0:T(8,128)S(1)} collective-permute-done((f32[2,6,256,256]{3,2,1,0:T(8,128)S(1)}, f32[2,6,256,256]{3,2,1,0:T(8,128)S(1)}, u32[]{:S(2)}, u32[]{:S(2)}) %collective-permute-start.5) | collective-permute-done | bytes 3145760 | tf_op jit(solution)/shard_map/ppermute | solution.py:24
  286.3 9.7 %fusion.4 = f32[2,6,256,256]{3,2,1,0:T(8,128)S(1)} fusion(f32[2,6,256,256]{3,2,1,0:T(8,128)} %copy-done.2, f32[2,6,256,256]{3,2,1,0:T(8,128)S(1)} %collective-permute-done.5, f32[2,6,256,256]{3,2,1,0:T(8,128)S(1)} %collective-permute-done.4), kind=kLoop, calls=%fused_computation.88 | loop fusion | flops 27525120 | bytes 12582912 | tf_op jit(solution)/shard_map/add | solution.py:34
  296.1 5.0 %multiply_add_fusion = f32[2,6,256,256]{3,2,1,0:T(8,128)S(1)} fusion(f32[2,6,256,256]{3,2,1,0:T(8,128)S(1)} %fusion.4), kind=kLoop, calls=%fused_computation.257 | loop fusion | flops 19660800 | bytes 6291456 | tf_op jit(solution)/shard_map/add | solution.py:34
  301.1 12.2 %multiply_reduce_fusion = (f32[6,256,256]{2,1,0:T(8,128)}, f32[2,6,256,256]{3,2,1,0:T(8,128)}) fusion(f32[2]{0:T(128)S(1)} %dynamic_slice.6, f32[2,6,256,256]{3,2,1,0:T(8,128)S(1)} %multiply_add_fusion, f32[2,6,256,256]{3,2,1,0:T(8,128)S(1)} %get-tuple-element.5, f32[2]{0:T(128)S(1)} %broadcast_multiply_fusion.2, f32[6,256,256]{2,1,0:T(8,128)S(1)} %exp.6), kind=kLoop, calls=%fused_computation.256 | loop fusion | flops 23199744 | bytes 12582928 | tf_op jit(solution)/shard_map/reduce_sum | solution.py:94
  313.4 54.6 %all-reduce.12.cloned.1.call-done = f32[6,256,256]{2,1,0:T(8,128)} async-done(((f32[6,256,256]{2,1,0:T(8,128)}), f32[6,256,256]{2,1,0:T(8,128)}) %all-reduce.12.cloned.1.call-update) | async-done | bytes 1572880 | tf_op jit(solution)/shard_map/psum | solution.py:95
  368.0 1.7 exp.7
  369.9 4.9 %multiply_divide_fusion = f32[2,6,256,256]{3,2,1,0:T(8,128)} fusion(f32[2,6,256,256]{3,2,1,0:T(8,128)} %get-tuple-element.3, f32[6,256,256]{2,1,0:T(8,128)S(1)} %exp.7, f32[2,6,256,256]{3,2,1,0:T(8,128)S(1)} %get-tuple-element.5, f32[2]{0:T(128)S(1)} %broadcast_multiply_fusion.2, f32[6,256,256]{2,1,0:T(8,128)S(1)} %copy-done.1), kind=kLoop, calls=%fused_computation.255 | loop fusion | flops 3145728 | bytes 12582920 | tf_op jit(solution)/shard_map/div | solution.py:96
  (33 shorter events, 8.0 us)
Async XLA Ops:
  7.2 175.5 %all-reduce.10.cloned.1.call-start = ((), (), s32[]{:S(2)}) async-start(), calls=%async_computation | async-start | bytes 3145728 | tf_op jit(solution)/shard_map/psum | solution.py:88
  9.7 9.5 %copy-start.4 = (f32[8]{0:T(128)S(1)}, f32[8]{0:T(128)}, u32[]{:S(2)}) copy-start(f32[8]{0:T(128)} %param.6) | copy-start | bytes 100
  9.7 10.1 %copy-start.5 = (u32[128]{0:T(128)S(1)}, u32[128]{0:T(128)}, u32[]{:S(2)}) copy-start(u32[128]{0:T(128)} %constant.60) | copy-start | bytes 1540
  12.3 98.0 %collective-permute-start.1 = (f32[2,6,256,256]{3,2,1,0:T(8,128)S(1)}, f32[2,6,256,256]{3,2,1,0:T(8,128)}, u32[]{:S(2)}, u32[]{:S(2)}) collective-permute-start(f32[2,6,256,256]{3,2,1,0:T(8,128)S(1)} %get-tuple-element.6), channel_id=1, source_target_pairs={{4,0},{8,4},{12,8},{16,12},{20,16},{24,20},{28,24},{32,28},{36,32}... | collective-permute-start | bytes 9437192 | tf_op jit(solution)/shard_map/ppermute | solution.py:24
  15.6 94.7 %collective-permute-start = (f32[2,6,256,256]{3,2,1,0:T(8,128)S(1)}, f32[2,6,256,256]{3,2,1,0:T(8,128)}, u32[]{:S(2)}, u32[]{:S(2)}) collective-permute-start(f32[2,6,256,256]{3,2,1,0:T(8,128)S(1)} %get-tuple-element.6), channel_id=1, source_target_pairs={{0,4},{4,8},{8,12},{12,16},{16,20},{20,24},{24,28},{28,32},{32,36}... | collective-permute-start | bytes 9437192 | tf_op jit(solution)/shard_map/ppermute | solution.py:22
  136.1 231.8 %all-reduce.12.cloned.1.call-start = ((), (), s32[]{:S(2)}) async-start(), calls=%async_computation.1 | async-start | bytes 3145728 | tf_op jit(solution)/shard_map/psum | solution.py:95
  184.3 116.8 %copy-start = (f32[6,256,256]{2,1,0:T(8,128)}, f32[6,256,256]{2,1,0:T(8,128)S(1)}, u32[]{:S(2)}) copy-start(f32[6,256,256]{2,1,0:T(8,128)S(1)} %exp.6) | copy-start | bytes 4718596
  185.0 38.8 %collective-permute-start.3 = (f32[2,6,256,256]{3,2,1,0:T(8,128)S(1)}, f32[2,6,256,256]{3,2,1,0:T(8,128)S(1)}, u32[]{:S(2)}, u32[]{:S(2)}) collective-permute-start(f32[2,6,256,256]{3,2,1,0:T(8,128)S(1)} %multiply_divide_fusion.1), channel_id=1, source_target_pairs={{4,0},{8,4},{12,8},{16,12},{20,16},{24,20},{28,24},{32,28},{36,32}... | collective-permute-start | bytes 9437192 | tf_op jit(solution)/shard_map/ppermute | solution.py:24
  187.7 37.3 %collective-permute-start.2 = (f32[2,6,256,256]{3,2,1,0:T(8,128)S(1)}, f32[2,6,256,256]{3,2,1,0:T(8,128)S(1)}, u32[]{:S(2)}, u32[]{:S(2)}) collective-permute-start(f32[2,6,256,256]{3,2,1,0:T(8,128)S(1)} %multiply_divide_fusion.1), channel_id=1, source_target_pairs={{0,4},{4,8},{8,12},{12,16},{16,20},{20,24},{24,28},{28,32},{32,36}... | collective-permute-start | bytes 9437192 | tf_op jit(solution)/shard_map/ppermute | solution.py:22
  245.8 39.4 %copy-start.2 = (f32[2,6,256,256]{3,2,1,0:T(8,128)}, f32[2,6,256,256]{3,2,1,0:T(8,128)S(1)}, u32[]{:S(2)}) copy-start(f32[2,6,256,256]{3,2,1,0:T(8,128)S(1)} %fusion.122) | copy-start | bytes 9437188
  245.8 39.3 %collective-permute-start.5 = (f32[2,6,256,256]{3,2,1,0:T(8,128)S(1)}, f32[2,6,256,256]{3,2,1,0:T(8,128)S(1)}, u32[]{:S(2)}, u32[]{:S(2)}) collective-permute-start(f32[2,6,256,256]{3,2,1,0:T(8,128)S(1)} %fusion.122), channel_id=1, source_target_pairs={{4,0},{8,4},{12,8},{16,12},{20,16},{24,20},{28,24},{32,28},{36,32}... | collective-permute-start | bytes 9437192 | tf_op jit(solution)/shard_map/ppermute | solution.py:24
  247.7 38.6 %collective-permute-start.4 = (f32[2,6,256,256]{3,2,1,0:T(8,128)S(1)}, f32[2,6,256,256]{3,2,1,0:T(8,128)S(1)}, u32[]{:S(2)}, u32[]{:S(2)}) collective-permute-start(f32[2,6,256,256]{3,2,1,0:T(8,128)S(1)} %fusion.122), channel_id=1, source_target_pairs={{0,4},{4,8},{8,12},{12,16},{16,20},{20,24},{24,28},{28,32},{32,36}... | collective-permute-start | bytes 9437192 | tf_op jit(solution)/shard_map/ppermute | solution.py:22
  368.0 1.9 copy-start.1
  369.7 5.0 %copy-start.3 = (f32[6,256,256]{2,1,0:T(8,128)}, f32[6,256,256]{2,1,0:T(8,128)S(1)}, u32[]{:S(2)}) copy-start(f32[6,256,256]{2,1,0:T(8,128)S(1)} %exp.7) | copy-start | bytes 4718596
Sparse Core Ops, SparseCore 0:
  136.3 46.3 all-reduce.9
  313.5 54.4 all-reduce.11
